TPU v7x, 256 devices: a whole 4x4x8 slice. The times are simulated.
256 devices in a mesh: pipe: 8 (over y, core), ctx: 32 (over x, z).
Axes of the slice: x: 4, y: 4, z: 8, core: 2. Of those that a mesh axis runs over, the one named last changes fastest.
Arguments:
- queries: bfloat16 [8, 4096, 4096], P('pipe', 'ctx'), may hold values from -240 to 240
- keys: bfloat16 [8, 4096, 4096], P('pipe', 'ctx'), may hold values from -6 to 6
- values: bfloat16 [8, 4096, 4096], P('pipe', 'ctx'), may hold values from -6 to 6
- attn_out: bfloat16 [8, 4096, 4096], P('pipe', 'ctx'), may hold values from -3 to 3
- out_grad: bfloat16 [8, 4096, 4096], P('pipe', 'ctx'), may hold values from -24 to 24
- random_blocks: int32 [8, 32, 64, 3], P('pipe', 'ctx'), may hold values from 0 to 63
- global_blocks: int32 [8, 2], P('pipe'), may hold values from 0 to 63, as said below
- radius: int32 [8, 32], P('pipe', 'ctx'), may hold values from 1 to 2, as said below
Outputs:
- grad_queries: bfloat16 [8, 4096, 4096], P('pipe', 'ctx')
- grad_keys: bfloat16 [8, 4096, 4096], P('pipe', 'ctx')
- grad_values: bfloat16 [8, 4096, 4096], P('pipe', 'ctx')
Inputs may be any that keep to these rules, and one draw needn't show every extreme that they name: `global_blocks`: the 2 entries of a section differ. In every section some head has radius 2 and some head has radius 1.
All inputs are finite; a program needn't handle non-finite values.
Results may differ from a plain program's by a relative error of at most 0.0049.
Values may be sent and summed in bfloat16 or wider, within the bound.
No kernel may reach another device: no remote copies, remote signals or barrier semaphores. Data moves between devices by JAX's collectives and lax.ppermute only.
A program may use at most 64 MiB of HBM per device.

v0:
```python
import jax
import jax.numpy as jnp
from jax import lax
from jax.sharding import PartitionSpec as P

HD = 128
BLK = 64
RMAX = 2
NR = 3
QG = 8
KB = 10


def passed_along(value, axis, steps):
    count = lax.axis_size(axis)
    pairs = [(source, (source + steps) % count) for source in range(count)]
    return lax.ppermute(value, axis, pairs)


def slot_table(random_list, global_list, head_radius, block_count):
    blocks = jnp.arange(block_count, dtype=jnp.int32)[:, None]
    offsets = jnp.arange(-RMAX, RMAX + 1, dtype=jnp.int32)[None, :]
    window = blocks + offsets
    window_ok = (jnp.abs(offsets) <= head_radius) & (window >= 0) & (window < block_count)
    window = jnp.clip(window, 0, block_count - 1)
    global_slots = jnp.broadcast_to(global_list[None, :], (block_count, global_list.shape[0]))
    global_ok = jnp.abs(global_slots - blocks) > head_radius
    random_ok = jnp.abs(random_list - blocks) > head_radius
    random_ok = random_ok & jnp.all(random_list[:, :, None] != global_list[None, None, :], axis=2)
    earlier = jnp.arange(NR)[None, :] < jnp.arange(NR)[:, None]
    repeated = jnp.any((random_list[:, :, None] == random_list[:, None, :]) & earlier[None], axis=2)
    random_ok = random_ok & jnp.logical_not(repeated)
    slot_index = jnp.concatenate([window, global_slots, random_list], axis=1)
    slot_valid = jnp.concatenate([window_ok, global_ok, random_ok], axis=1)
    return (slot_index, slot_valid)


def lane_sums(first, second):
    product = first.astype(jnp.float32) * second.astype(jnp.float32)
    flat = product.reshape(-1, product.shape[-1])
    ones_column = jnp.ones((product.shape[-1],), jnp.float32)
    summed = jnp.dot(
        flat, ones_column, precision=lax.Precision.HIGHEST, preferred_element_type=jnp.float32
    )
    return summed.reshape(product.shape[:-1])


def head_grads(
    query_rows,
    key_rows,
    value_rows,
    grad_rows,
    correction_rows,
    random_list,
    global_list,
    head_radius,
):
    block_count = query_rows.shape[0] // BLK
    score_scale = HD ** (-0.5)
    slot_index, slot_valid = slot_table(random_list, global_list, head_radius, block_count)
    query_blocks = query_rows.reshape(block_count, BLK, HD)
    key_blocks = key_rows.reshape(block_count, BLK, HD)
    value_blocks = value_rows.reshape(block_count, BLK, HD)
    grad_blocks = grad_rows.reshape(block_count, BLK, HD)
    correction = correction_rows.reshape(block_count, BLK)
    block_ids = jnp.arange(block_count, dtype=jnp.int32)[:, None]

    def one_group(totals, first_block):
        key_total, value_total = totals
        group_index = lax.dynamic_slice_in_dim(slot_index, first_block, QG, 0)
        group_valid = lax.dynamic_slice_in_dim(slot_valid, first_block, QG, 0)
        group_query = lax.dynamic_slice_in_dim(query_blocks, first_block, QG, 0)
        group_grad = lax.dynamic_slice_in_dim(grad_blocks, first_block, QG, 0)
        group_corr = lax.dynamic_slice_in_dim(correction, first_block, QG, 0)
        key_tiles = key_blocks[group_index].reshape(QG, KB * BLK, HD)
        value_tiles = value_blocks[group_index].reshape(QG, KB * BLK, HD)
        key_live = jnp.repeat(group_valid, BLK, axis=1)
        scores = (
            jnp.einsum("bid,bjd->bij", group_query, key_tiles, preferred_element_type=jnp.float32)
            * score_scale
        )
        scores = jnp.where(key_live[:, None, :], scores, -jnp.inf)
        row_max = jnp.max(scores, axis=-1, keepdims=True)
        weights = jnp.exp(scores - row_max)
        attention = weights / jnp.sum(weights, axis=-1, keepdims=True)
        attention_low = attention.astype(jnp.bfloat16)
        dprobs = jnp.einsum(
            "bid,bjd->bij", group_grad, value_tiles, preferred_element_type=jnp.float32
        )
        dscores_low = (attention * (dprobs - group_corr[:, :, None])).astype(jnp.bfloat16)
        query_grad = (
            jnp.einsum("bij,bjd->bid", dscores_low, key_tiles, preferred_element_type=jnp.float32)
            * score_scale
        ).astype(jnp.bfloat16)
        key_part = jnp.einsum(
            "bij,bid->bjd", dscores_low, group_query, preferred_element_type=jnp.float32
        ).reshape(QG * KB, BLK * HD)
        value_part = jnp.einsum(
            "bij,bid->bjd", attention_low, group_grad, preferred_element_type=jnp.float32
        ).reshape(QG * KB, BLK * HD)
        flat_index = group_index.reshape(1, -1)
        placing = (block_ids == flat_index).astype(jnp.float32)
        key_total = key_total + jnp.dot(
            placing, key_part, precision=lax.Precision.HIGHEST, preferred_element_type=jnp.float32
        )
        value_total = value_total + jnp.dot(
            placing, value_part, precision=lax.Precision.HIGHEST, preferred_element_type=jnp.float32
        )
        return ((key_total, value_total), query_grad)

    starts = jnp.arange(block_count // QG) * QG
    empty = jnp.zeros((block_count, BLK * HD), jnp.float32)
    (key_total, value_total), query_grad = lax.scan(one_group, (empty, empty), starts)
    query_grad = query_grad.reshape(block_count * BLK, HD)
    key_grad = (key_total * score_scale).astype(jnp.bfloat16).reshape(block_count * BLK, HD)
    value_grad = value_total.astype(jnp.bfloat16).reshape(block_count * BLK, HD)
    return (query_grad, key_grad, value_grad)


def body(queries, keys, values, attn_out, out_grad, random_blocks, global_blocks, radius):
    head_query, head_key, head_value, head_output, head_grad = (
        lax.all_to_all(queries, "ctx", split_axis=2, concat_axis=1, tiled=True),
        lax.all_to_all(keys, "ctx", split_axis=2, concat_axis=1, tiled=True),
        lax.all_to_all(values, "ctx", split_axis=2, concat_axis=1, tiled=True),
        lax.all_to_all(attn_out, "ctx", split_axis=2, concat_axis=1, tiled=True),
        lax.all_to_all(out_grad, "ctx", split_axis=2, concat_axis=1, tiled=True),
    )
    length = head_query.shape[1]
    local_heads = head_query.shape[2] // HD
    correction = lane_sums(
        head_output.reshape(1, length, local_heads, HD),
        head_grad.reshape(1, length, local_heads, HD),
    )
    local_heads = head_query.shape[2] // HD
    columns = slice(0, HD)
    query_grad, key_grad, value_grad = head_grads(
        head_query[0, :, columns],
        head_key[0, :, columns],
        head_value[0, :, columns],
        head_grad[0, :, columns],
        correction[0, :, 0],
        random_blocks[0, 0],
        global_blocks[0],
        radius[0, 0],
    )
    gradients = jnp.stack([query_grad, key_grad, value_grad], axis=0)[:, None]
    returned = lax.all_to_all(gradients, "ctx", split_axis=2, concat_axis=3, tiled=True)
    arrived = passed_along(returned, "pipe", -1)
    return (arrived[0], arrived[1], arrived[2])


def solution(mesh):
    return jax.shard_map(
        body,
        mesh=mesh,
        in_specs=(
            P("pipe", "ctx", None),
            P("pipe", "ctx", None),
            P("pipe", "ctx", None),
            P("pipe", "ctx", None),
            P("pipe", "ctx", None),
            P("pipe", "ctx", None, None),
            P("pipe", None),
            P("pipe", "ctx"),
        ),
        out_specs=(P("pipe", "ctx", None), P("pipe", "ctx", None), P("pipe", "ctx", None)),
        check_vma=False,
    )
```

profile of v0, /device:TPU:1, one launch (start us, length us, event | category | flops | bytes accessed | tf_op | source)
XLA Modules:
  0.0 691.4 jit_solution(3119696237251115099)
XLA Ops:
  0.6 5.0 copy.91
  6.2 22.3 %reduce = bf16[4096,128]{1,0:T(8,128)(2,1)S(1)} reduce(bf16[4096,1,128]{2,1,0:T(2,128)(2,1)S(1)} %bitcast.108, bf16[]{:T(256)} %broadcast.74), dimensions={1}, to_apply=%bitcast.48.reduce_sub_computation | reduce | bytes 2097154
  29.6 11.9 %all-to-all-start = ((bf16[32,2,8192]{2,1,0:T(2,128)(2,1)}), bf16[32,2,8192]{2,1,0:T(2,128)(2,1)S(1)}, u32[]{:S(2)}, u32[]{:S(2)}) async-start(bf16[32,2,8192]{2,1,0:T(2,128)(2,1)} %reshape.110), calls=%async_computation | async-start | bytes 2097152 | tf_op jit(solution)/shard_map/all_to_all | solution.py:122
  41.5 5.0 copy.93
  46.5 23.3 %reduce.1 = bf16[4096,128]{1,0:T(8,128)(2,1)} reduce(bf16[4096,1,128]{2,1,0:T(2,128)(2,1)S(1)} %bitcast.111, bf16[]{:T(256)} %broadcast.74), dimensions={1}, to_apply=%bitcast.50.reduce_sub_computation | reduce | bytes 2097154
  72.0 9.8 %all-to-all-start.1 = ((bf16[32,2,8192]{2,1,0:T(2,128)(2,1)}), bf16[32,2,8192]{2,1,0:T(2,128)(2,1)}, u32[]{:S(2)}, u32[]{:S(2)}) async-start(bf16[32,2,8192]{2,1,0:T(2,128)(2,1)} %reshape.112), calls=%async_computation.1 | async-start | bytes 2097152 | tf_op jit(solution)/shard_map/all_to_all | solution.py:123
  81.8 5.0 copy.97
  86.8 23.3 %reduce.3 = bf16[4096,128]{1,0:T(8,128)(2,1)} reduce(bf16[4096,1,128]{2,1,0:T(2,128)(2,1)S(1)} %bitcast.112, bf16[]{:T(256)} %broadcast.74), dimensions={1}, to_apply=%bitcast.54.reduce_sub_computation | reduce | bytes 2097154
  112.2 9.5 %all-to-all-start.3 = ((bf16[32,2,8192]{2,1,0:T(2,128)(2,1)}), bf16[32,2,8192]{2,1,0:T(2,128)(2,1)}, u32[]{:S(2)}, u32[]{:S(2)}) async-start(bf16[32,2,8192]{2,1,0:T(2,128)(2,1)} %reshape.116), calls=%async_computation.3 | async-start | bytes 2097152 | tf_op jit(solution)/shard_map/all_to_all | solution.py:124
  121.7 5.0 copy.99
  126.8 23.3 %reduce.4 = bf16[4096,128]{1,0:T(8,128)(2,1)} reduce(bf16[4096,1,128]{2,1,0:T(2,128)(2,1)S(1)} %bitcast.113, bf16[]{:T(256)} %broadcast.74), dimensions={1}, to_apply=%bitcast.56.reduce_sub_computation | reduce | bytes 2097154
  152.2 9.5 %all-to-all-start.4 = ((bf16[32,2,8192]{2,1,0:T(2,128)(2,1)}), bf16[32,2,8192]{2,1,0:T(2,128)(2,1)}, u32[]{:S(2)}, u32[]{:S(2)}) async-start(bf16[32,2,8192]{2,1,0:T(2,128)(2,1)} %reshape.118), calls=%async_computation.4 | async-start | bytes 2097152 | tf_op jit(solution)/shard_map/all_to_all | solution.py:125
  162.4 5.0 copy.95
  167.4 23.3 %reduce.2 = bf16[4096,128]{1,0:T(8,128)(2,1)} reduce(bf16[4096,1,128]{2,1,0:T(2,128)(2,1)S(1)} %bitcast.109, bf16[]{:T(256)} %broadcast.74), dimensions={1}, to_apply=%bitcast.52.reduce_sub_computation | reduce | bytes 2097154
  193.1 9.5 %all-to-all-start.2 = ((bf16[32,2,8192]{2,1,0:T(2,128)(2,1)}), bf16[32,2,8192]{2,1,0:T(2,128)(2,1)}, u32[]{:S(2)}, u32[]{:S(2)}) async-start(bf16[32,2,8192]{2,1,0:T(2,128)(2,1)} %reshape.114), calls=%async_computation.2 | async-start | bytes 2097152 | tf_op jit(solution)/shard_map/all_to_all | solution.py:126
  234.2 6.2 fusion.25
  240.4 274.9 %while.15 = (s32[]{:T(128)}, f32[64,8192]{1,0:T(8,128)}, f32[64,8192]{1,0:T(8,128)}, bf16[8,8,64,128]{3,2,1,0:T(8,128)(2,1)}, s32[8]{0:T(128)S(1)}, /*index=5*/s...) while((s32[]{:T(128)}, f32[64,8192]{1,0:T(8,128)}, ...), condition=%wide.region_5.6_spmd.clone, body=%wide.region_2.5_spmd.clone.sunk | while | flops 1431909376 | bytes 54307064 | solution.py:113
  292.4 4.4 convolution_add_fusion.5
  302.5 4.4 convolution_add_fusion.4
  327.1 4.4 convolution_add_fusion.5
  337.2 4.4 convolution_add_fusion.4
  361.9 4.4 convolution_add_fusion.5
  371.9 4.4 convolution_add_fusion.4
  396.6 4.4 convolution_add_fusion.5
  431.3 4.4 convolution_add_fusion.5
  466.1 4.4 convolution_add_fusion.5
  500.8 4.4 convolution_add_fusion.5
  510.9 4.4 convolution_add_fusion.4
  521.4 20.0 %copy.103 = bf16[3,1,4096,128]{3,0,1,2:T(4,128)(2,1)S(1)} copy(bf16[3,1,4096,128]{3,2,0,1:T(8,128)(2,1)S(1)} %maximum_bitcast_fusion) | data formatting | bytes 6291456 | tf_op jit(solution)/shard_map/broadcast_in_dim | solution.py:146
  541.4 98.1 %all_to_all.87 = bf16[3,1,4096,128]{3,0,1,2:T(4,128)(2,1)S(1)} all-to-all(bf16[3,1,4096,128]{3,0,1,2:T(4,128)(2,1)S(1)} %copy.103), channel_id=1, replica_groups=mesh['pipe'=8,'ctx'=32] {'ctx'}, dimensions={2} | all-to-all | bytes 6291456 | tf_op jit(solution)/shard_map/all_to_all | solution.py:147
  642.8 7.9 %collective-permute-start = (bf16[3,1,128,4096]{2,3,0,1:T(8,128)(2,1)}, bf16[3,1,128,4096]{2,3,0,1:T(8,128)(2,1)S(1)}, u32[]{:S(2)}, u32[]{:S(2)}) collective-permute-start(bf16[3,1,128,4096]{2,3,0,1:T(8,128)(2,1)} %bitcast.119), channel_id=1, source_target_pairs={{0,224},{32,0},{64,32},{96,64},{128,96},{160,128},{192,160},{224,1... | collective-permute-start | bytes 9437192 | tf_op jit(solution)/shard_map/ppermute | solution.py:17
  650.7 36.4 %collective-permute-done = bf16[3,1,128,4096]{2,3,0,1:T(8,128)(2,1)S(1)} collective-permute-done((bf16[3,1,128,4096]{2,3,0,1:T(8,128)(2,1)}, bf16[3,1,128,4096]{2,3,0,1:T(8,128)(2,1)S(1)}, u32[]{:S(2)}, u32[]{:S(2)}) %collective-permute-start) | collective-permute-done | bytes 3145760 | tf_op jit(solution)/shard_map/ppermute | solution.py:17
  (239 shorter events, 265.5 us)
Async XLA Ops:
  29.6 42.3 %all-to-all-start = ((bf16[32,2,8192]{2,1,0:T(2,128)(2,1)}), bf16[32,2,8192]{2,1,0:T(2,128)(2,1)S(1)}, u32[]{:S(2)}, u32[]{:S(2)}) async-start(bf16[32,2,8192]{2,1,0:T(2,128)(2,1)} %reshape.110), calls=%async_computation | async-start | bytes 2097152 | tf_op jit(solution)/shard_map/all_to_all | solution.py:122
  72.0 40.3 %all-to-all-start.1 = ((bf16[32,2,8192]{2,1,0:T(2,128)(2,1)}), bf16[32,2,8192]{2,1,0:T(2,128)(2,1)}, u32[]{:S(2)}, u32[]{:S(2)}) async-start(bf16[32,2,8192]{2,1,0:T(2,128)(2,1)} %reshape.112), calls=%async_computation.1 | async-start | bytes 2097152 | tf_op jit(solution)/shard_map/all_to_all | solution.py:123
  112.2 40.0 %all-to-all-start.3 = ((bf16[32,2,8192]{2,1,0:T(2,128)(2,1)}), bf16[32,2,8192]{2,1,0:T(2,128)(2,1)}, u32[]{:S(2)}, u32[]{:S(2)}) async-start(bf16[32,2,8192]{2,1,0:T(2,128)(2,1)} %reshape.116), calls=%async_computation.3 | async-start | bytes 2097152 | tf_op jit(solution)/shard_map/all_to_all | solution.py:124
  150.1 12.3 %copy-start.4 = (s32[1,1,64,3]{2,1,3,0:T(1,128)S(1)}, s32[1,1,64,3]{2,1,3,0:T(1,128)}, u32[]{:S(2)}) copy-start(s32[1,1,64,3]{2,1,3,0:T(1,128)} %param.15) | copy-start | bytes 2308
  152.2 40.8 %all-to-all-start.4 = ((bf16[32,2,8192]{2,1,0:T(2,128)(2,1)}), bf16[32,2,8192]{2,1,0:T(2,128)(2,1)}, u32[]{:S(2)}, u32[]{:S(2)}) async-start(bf16[32,2,8192]{2,1,0:T(2,128)(2,1)} %reshape.118), calls=%async_computation.4 | async-start | bytes 2097152 | tf_op jit(solution)/shard_map/all_to_all | solution.py:125
  167.4 25.6 %copy-start.5 = (s32[1,2]{1,0:T(1,128)S(1)}, s32[1,2]{1,0:T(1,128)}, u32[]{:S(2)}) copy-start(s32[1,2]{1,0:T(1,128)} %param.16) | copy-start | bytes 28
  193.1 34.7 %all-to-all-start.2 = ((bf16[32,2,8192]{2,1,0:T(2,128)(2,1)}), bf16[32,2,8192]{2,1,0:T(2,128)(2,1)}, u32[]{:S(2)}, u32[]{:S(2)}) async-start(bf16[32,2,8192]{2,1,0:T(2,128)(2,1)} %reshape.114), calls=%async_computation.2 | async-start | bytes 2097152 | tf_op jit(solution)/shard_map/all_to_all | solution.py:126
  232.2 2.0 copy-start.2
  250.2 1.5 copy-start.1
  281.8 1.5 copy-start.1
  316.5 1.5 copy-start.1
  351.2 1.5 copy-start.1
  386.0 1.5 copy-start.1
  420.7 1.5 copy-start.1
  455.4 1.5 copy-start.1
  490.2 1.5 copy-start.1
  515.3 3.2 copy-start
  518.6 1.2 copy-start.3
  642.8 44.3 %collective-permute-start = (bf16[3,1,128,4096]{2,3,0,1:T(8,128)(2,1)}, bf16[3,1,128,4096]{2,3,0,1:T(8,128)(2,1)S(1)}, u32[]{:S(2)}, u32[]{:S(2)}) collective-permute-start(bf16[3,1,128,4096]{2,3,0,1:T(8,128)(2,1)} %bitcast.119), channel_id=1, source_target_pairs={{0,224},{32,0},{64,32},{96,64},{128,96},{160,128},{192,160},{224,1... | collective-permute-start | bytes 9437192 | tf_op jit(solution)/shard_map/ppermute | solution.py:17
where the time goes:
time: 704 us; the launch traced here: 691 us
  local copies, waits for them, and re-layouts  184 us (26%)
  matrix products  162 us (23%)
  other arithmetic  135 us (19%)
  blocking collectives  98.1 us (14%)
  starting transfers between devices  58 us (8%)
  waiting for transfers between devices  36.4 us (5%)
  loops' own time  16.2 us (2%)
    unnamed x7, other arithmetic  116 us
    all_to_all x1, blocking collectives, body(): lax.all_to_all(gradients, 'ctx', split_axis=2, concat_axis=3, tiled=True)  98.1 us
    unnamed x36, local copies, waits for them, and re-layouts  59.7 us
    ppermute x1, waiting for transfers between devices, passed_along(): return lax.ppermute(value, axis, pairs)  36.4 us
    dot_general x8, matrix products, one_group(): jnp.dot(placing, value_part, precision=lax.Precision.HIGHEST, preferred_e...  34 us
    dot_general x8, matrix products, one_group(): jnp.dot(placing, key_part, precision=lax.Precision.HIGHEST, preferred_ele...  33.5 us
    dot_general x8, matrix products, one_group(): jnp.einsum('bij,bid->bjd', attention_low, group_grad, preferred_element_t...  31.2 us
    gather x8, local copies, waits for them, and re-layouts, one_group(): value_tiles = value_blocks[group_index].reshape(QG, KB * BLK, HD)  24.8 us
  transfers between devices with their start and end apart: 6, of which 1 were waited for; matrix products, arithmetic and copies ran while one was open for 21% of the time, Pallas kernels for 0%

commit v1 on v0

--- a/solution.py
+++ b/solution.py
@@ -2,6 +2,7 @@
 import jax.numpy as jnp
 from jax import lax
 from jax.sharding import PartitionSpec as P
+from jax.lax import all_to_all, axis_size
 
 HD = 128
 BLK = 64
@@ -144,7 +145,11 @@
         radius[0, 0],
     )
     gradients = jnp.stack([query_grad, key_grad, value_grad], axis=0)[:, None]
-    returned = lax.all_to_all(gradients, "ctx", split_axis=2, concat_axis=3, tiled=True)
+    placed = axis_size("ctx")
+    t1 = jnp.split(gradients, placed, axis=2)
+    s_next = jnp.stack(t1)
+    top = all_to_all(s_next, "ctx", split_axis=0, concat_axis=0)
+    returned = jnp.concatenate(top, axis=3)
     arrived = passed_along(returned, "pipe", -1)
     return (arrived[0], arrived[1], arrived[2])
 

time: 704 us -> 665 us (0.945)
  blocking collectives: 98.1 us -> 75.6 us
  local copies, waits for them, and re-layouts: 184 us -> 163 us
    all_to_all x1, blocking collectives: 98.1 us -> 75.6 us  [body(): top = all_to_all(s_next, 'ctx', split_axis=0, concat_axis=0)]
    broadcast_in_dim x1 -> x0, local copies, waits for them, and re-layouts: 20 us -> none  [body(): gradients = jnp.stack([query_grad, key_grad, value_grad], axis=0)[:, None]]
    unnamed x36 -> x65, local copies, waits for them, and re-layouts: 59.7 us -> 59.4 us
  transfers between devices with their start and end apart: 6 -> 6, of which waited for: 1 -> 1; matrix products, arithmetic and copies ran while one was open for 21% -> 23% of each run, Pallas kernels for 0% -> 0%
where the time goes in v1:
time: 665 us; the launch traced here: 653 us
  matrix products  166 us (25%)
  local copies, waits for them, and re-layouts  163 us (25%)
  other arithmetic  135 us (20%)
  blocking collectives  75.6 us (11%)
  starting transfers between devices  58 us (9%)
  waiting for transfers between devices  36.4 us (5%)
  loops' own time  16.1 us (2%)
    unnamed x7, other arithmetic  116 us
    all_to_all x1, blocking collectives, body(): top = all_to_all(s_next, 'ctx', split_axis=0, concat_axis=0)  75.6 us
    unnamed x65, local copies, waits for them, and re-layouts  59.4 us
    ppermute x1, waiting for transfers between devices, passed_along(): return lax.ppermute(value, axis, pairs)  36.3 us
    dot_general x8, matrix products, one_group(): jnp.dot(placing, value_part, precision=lax.Precision.HIGHEST, preferred_e...  34 us
    dot_general x8, matrix products, one_group(): jnp.dot(placing, key_part, precision=lax.Precision.HIGHEST, preferred_ele...  33.5 us
    dot_general x8, matrix products, one_group(): jnp.einsum('bij,bid->bjd', attention_low, group_grad, preferred_element_t...  31.2 us
    gather x8, local copies, waits for them, and re-layouts, one_group(): value_tiles = value_blocks[group_index].reshape(QG, KB * BLK, HD)  24.8 us
  transfers between devices with their start and end apart: 6, of which 1 were waited for; matrix products, arithmetic and copies ran while one was open for 23% of the time, Pallas kernels for 0%

profile of v1, /device:TPU:1, one launch (start us, length us, event | category | flops | bytes accessed | tf_op | source)
XLA Modules:
  0.0 652.8 jit_solution(6998634171446921796)
XLA Ops:
  0.6 5.0 copy.117
  6.2 22.3 %reduce = bf16[4096,128]{1,0:T(8,128)(2,1)S(1)} reduce(bf16[4096,1,128]{2,1,0:T(2,128)(2,1)S(1)} %bitcast.234, bf16[]{:T(256)} %broadcast.74), dimensions={1}, to_apply=%bitcast.174.reduce_sub_computation | reduce | bytes 2097154
  29.6 11.9 %all-to-all-start = ((bf16[32,2,8192]{2,1,0:T(2,128)(2,1)}), bf16[32,2,8192]{2,1,0:T(2,128)(2,1)S(1)}, u32[]{:S(2)}, u32[]{:S(2)}) async-start(bf16[32,2,8192]{2,1,0:T(2,128)(2,1)} %reshape.118), calls=%async_computation | async-start | bytes 2097152 | tf_op jit(solution)/shard_map/all_to_all | solution.py:123
  41.5 5.0 copy.119
  46.5 23.3 %reduce.1 = bf16[4096,128]{1,0:T(8,128)(2,1)} reduce(bf16[4096,1,128]{2,1,0:T(2,128)(2,1)S(1)} %bitcast.237, bf16[]{:T(256)} %broadcast.74), dimensions={1}, to_apply=%bitcast.176.reduce_sub_computation | reduce | bytes 2097154
  72.0 9.8 %all-to-all-start.1 = ((bf16[32,2,8192]{2,1,0:T(2,128)(2,1)}), bf16[32,2,8192]{2,1,0:T(2,128)(2,1)}, u32[]{:S(2)}, u32[]{:S(2)}) async-start(bf16[32,2,8192]{2,1,0:T(2,128)(2,1)} %reshape.120), calls=%async_computation.1 | async-start | bytes 2097152 | tf_op jit(solution)/shard_map/all_to_all | solution.py:124
  81.8 5.0 copy.123
  86.8 23.3 %reduce.3 = bf16[4096,128]{1,0:T(8,128)(2,1)} reduce(bf16[4096,1,128]{2,1,0:T(2,128)(2,1)S(1)} %bitcast.238, bf16[]{:T(256)} %broadcast.74), dimensions={1}, to_apply=%bitcast.180.reduce_sub_computation | reduce | bytes 2097154
  112.2 9.5 %all-to-all-start.3 = ((bf16[32,2,8192]{2,1,0:T(2,128)(2,1)}), bf16[32,2,8192]{2,1,0:T(2,128)(2,1)}, u32[]{:S(2)}, u32[]{:S(2)}) async-start(bf16[32,2,8192]{2,1,0:T(2,128)(2,1)} %reshape.124), calls=%async_computation.3 | async-start | bytes 2097152 | tf_op jit(solution)/shard_map/all_to_all | solution.py:125
  121.7 5.0 copy.125
  126.8 23.3 %reduce.4 = bf16[4096,128]{1,0:T(8,128)(2,1)} reduce(bf16[4096,1,128]{2,1,0:T(2,128)(2,1)S(1)} %bitcast.239, bf16[]{:T(256)} %broadcast.74), dimensions={1}, to_apply=%bitcast.182.reduce_sub_computation | reduce | bytes 2097154
  152.2 9.5 %all-to-all-start.4 = ((bf16[32,2,8192]{2,1,0:T(2,128)(2,1)}), bf16[32,2,8192]{2,1,0:T(2,128)(2,1)}, u32[]{:S(2)}, u32[]{:S(2)}) async-start(bf16[32,2,8192]{2,1,0:T(2,128)(2,1)} %reshape.126), calls=%async_computation.4 | async-start | bytes 2097152 | tf_op jit(solution)/shard_map/all_to_all | solution.py:126
  162.4 5.0 copy.121
  167.4 23.3 %reduce.2 = bf16[4096,128]{1,0:T(8,128)(2,1)} reduce(bf16[4096,1,128]{2,1,0:T(2,128)(2,1)S(1)} %bitcast.235, bf16[]{:T(256)} %broadcast.74), dimensions={1}, to_apply=%bitcast.178.reduce_sub_computation | reduce | bytes 2097154
  193.1 9.5 %all-to-all-start.2 = ((bf16[32,2,8192]{2,1,0:T(2,128)(2,1)}), bf16[32,2,8192]{2,1,0:T(2,128)(2,1)}, u32[]{:S(2)}, u32[]{:S(2)}) async-start(bf16[32,2,8192]{2,1,0:T(2,128)(2,1)} %reshape.122), calls=%async_computation.2 | async-start | bytes 2097152 | tf_op jit(solution)/shard_map/all_to_all | solution.py:127
  234.2 6.2 fusion.25
  240.4 278.8 %while.15 = (s32[]{:T(128)}, f32[64,8192]{1,0:T(8,128)}, f32[64,8192]{1,0:T(8,128)}, bf16[8,8,64,128]{3,2,1,0:T(8,128)(2,1)}, s32[8]{0:T(128)S(1)}, /*index=5*/s...) while((s32[]{:T(128)}, f32[64,8192]{1,0:T(8,128)}, ...), condition=%wide.region_5.6_spmd.clone, body=%wide.region_2.5_spmd.clone.sunk | while | flops 1431909376 | bytes 49064156 | solution.py:114
  293.4 4.4 convolution_add_fusion.5
  303.5 4.4 convolution_add_fusion.4
  328.6 4.4 convolution_add_fusion.5
  338.7 4.4 convolution_add_fusion.4
  363.8 4.4 convolution_add_fusion.5
  399.1 4.4 convolution_add_fusion.5
  409.1 4.4 convolution_add_fusion.4
  434.3 4.4 convolution_add_fusion.5
  444.4 4.4 convolution_add_fusion.4
  469.5 4.4 convolution_add_fusion.5
  479.6 4.4 convolution_add_fusion.4
  504.7 4.4 convolution_add_fusion.5
  525.7 75.6 %all_to_all.74 = bf16[32,3,1,128,128]{4,3,1,2,0:T(8,128)(2,1)S(1)} all-to-all(bf16[32,3,1,128,128]{4,3,1,2,0:T(8,128)(2,1)S(1)} %fusion.28), channel_id=1, replica_groups=mesh['pipe'=8,'ctx'=32] {'ctx'}, dimensions={0} | all-to-all | bytes 6291456 | tf_op jit(solution)/shard_map/all_to_all | solution.py:151
  604.2 7.9 %collective-permute-start = (bf16[3,1,128,4096]{2,3,0,1:T(8,128)(2,1)}, bf16[3,1,128,4096]{2,3,0,1:T(8,128)(2,1)S(1)}, u32[]{:S(2)}, u32[]{:S(2)}) collective-permute-start(bf16[3,1,128,4096]{2,3,0,1:T(8,128)(2,1)} %bitcast.245), channel_id=1, source_target_pairs={{0,224},{32,0},{64,32},{96,64},{128,96},{160,128},{192,160},{224,1... | collective-permute-start | bytes 9437192 | tf_op jit(solution)/shard_map/ppermute | solution.py:18
  612.1 36.3 %collective-permute-done = bf16[3,1,128,4096]{2,3,0,1:T(8,128)(2,1)S(1)} collective-permute-done((bf16[3,1,128,4096]{2,3,0,1:T(8,128)(2,1)}, bf16[3,1,128,4096]{2,3,0,1:T(8,128)(2,1)S(1)}, u32[]{:S(2)}, u32[]{:S(2)}) %collective-permute-start) | collective-permute-done | bytes 3145760 | tf_op jit(solution)/shard_map/ppermute | solution.py:18
  (251 shorter events, 264.8 us)
Async XLA Ops:
  29.6 42.3 %all-to-all-start = ((bf16[32,2,8192]{2,1,0:T(2,128)(2,1)}), bf16[32,2,8192]{2,1,0:T(2,128)(2,1)S(1)}, u32[]{:S(2)}, u32[]{:S(2)}) async-start(bf16[32,2,8192]{2,1,0:T(2,128)(2,1)} %reshape.118), calls=%async_computation | async-start | bytes 2097152 | tf_op jit(solution)/shard_map/all_to_all | solution.py:123
  72.0 40.3 %all-to-all-start.1 = ((bf16[32,2,8192]{2,1,0:T(2,128)(2,1)}), bf16[32,2,8192]{2,1,0:T(2,128)(2,1)}, u32[]{:S(2)}, u32[]{:S(2)}) async-start(bf16[32,2,8192]{2,1,0:T(2,128)(2,1)} %reshape.120), calls=%async_computation.1 | async-start | bytes 2097152 | tf_op jit(solution)/shard_map/all_to_all | solution.py:124
  112.2 40.0 %all-to-all-start.3 = ((bf16[32,2,8192]{2,1,0:T(2,128)(2,1)}), bf16[32,2,8192]{2,1,0:T(2,128)(2,1)}, u32[]{:S(2)}, u32[]{:S(2)}) async-start(bf16[32,2,8192]{2,1,0:T(2,128)(2,1)} %reshape.124), calls=%async_computation.3 | async-start | bytes 2097152 | tf_op jit(solution)/shard_map/all_to_all | solution.py:125
  126.8 35.6 %copy-start.2 = (s32[1,1,64,3]{2,1,3,0:T(1,128)S(1)}, s32[1,1,64,3]{2,1,3,0:T(1,128)}, u32[]{:S(2)}) copy-start(s32[1,1,64,3]{2,1,3,0:T(1,128)} %param.15) | copy-start | bytes 2308
  152.2 40.8 %all-to-all-start.4 = ((bf16[32,2,8192]{2,1,0:T(2,128)(2,1)}), bf16[32,2,8192]{2,1,0:T(2,128)(2,1)}, u32[]{:S(2)}, u32[]{:S(2)}) async-start(bf16[32,2,8192]{2,1,0:T(2,128)(2,1)} %reshape.126), calls=%async_computation.4 | async-start | bytes 2097152 | tf_op jit(solution)/shard_map/all_to_all | solution.py:126
  167.4 25.6 %copy-start.3 = (s32[1,2]{1,0:T(1,128)S(1)}, s32[1,2]{1,0:T(1,128)}, u32[]{:S(2)}) copy-start(s32[1,2]{1,0:T(1,128)} %param.16) | copy-start | bytes 28
  193.1 34.7 %all-to-all-start.2 = ((bf16[32,2,8192]{2,1,0:T(2,128)(2,1)}), bf16[32,2,8192]{2,1,0:T(2,128)(2,1)}, u32[]{:S(2)}, u32[]{:S(2)}) async-start(bf16[32,2,8192]{2,1,0:T(2,128)(2,1)} %reshape.122), calls=%async_computation.2 | async-start | bytes 2097152 | tf_op jit(solution)/shard_map/all_to_all | solution.py:127
  232.2 2.0 copy-start.1
  519.2 3.2 copy-start
  604.2 44.2 %collective-permute-start = (bf16[3,1,128,4096]{2,3,0,1:T(8,128)(2,1)}, bf16[3,1,128,4096]{2,3,0,1:T(8,128)(2,1)S(1)}, u32[]{:S(2)}, u32[]{:S(2)}) collective-permute-start(bf16[3,1,128,4096]{2,3,0,1:T(8,128)(2,1)} %bitcast.245), channel_id=1, source_target_pairs={{0,224},{32,0},{64,32},{96,64},{128,96},{160,128},{192,160},{224,1... | collective-permute-start | bytes 9437192 | tf_op jit(solution)/shard_map/ppermute | solution.py:18
